TPU v7x, 512 devices: a whole 4x4x16 slice. The times are simulated.
512 devices in a mesh: gx: 32 (over z_hi, x, core), gy: 4 (over y), gz: 4 (over z_lo).
Axes of the slice: x: 4, y: 4, z: 16 (z_hi: 4, z_lo: 4; z = z_hi * 4 + z_lo), core: 2. Of those that a mesh axis runs over, the one named last changes fastest.
Arguments:
- level_set: float32 [1024, 128, 512], P('gx', 'gy', 'gz'), may hold values from -6 to 6
- velocity: bfloat16 [3, 1024, 128, 512], P(None, 'gx', 'gy', 'gz'), may hold values from -1 to 1
- active_brick: int32 [32, 4, 4], P('gx', 'gy', 'gz'), may hold values 0 or 1
- depth_order: int32 [4], replicated, may hold values from 0 to 3, as said below
Outputs:
- level_out: float32 [1024, 128, 512], P('gx', 'gy', 'gz')
- image: float32 [4, 2048, 256], P(None, ('gx', 'gz'), 'gy')
Inputs may be any that keep to these rules, and one draw needn't show every extreme that they name: `depth_order`: either 0, 1, .. in slab order or the reverse.
All inputs are finite; a program needn't handle non-finite values. No bound on the sum of `active_brick` on one device may be relied on, other than what follows from the above.
Results may differ from a plain program's by a relative error of at most 0.0003.
Values may be sent and summed in bfloat16 or wider, within the bound.
No kernel may reach another device: no remote copies, remote signals or barrier semaphores. Data moves between devices by JAX's collectives and lax.ppermute only.
A program may use at most 64 MiB of HBM per device.

v0:
```python
import jax
import jax.numpy as jnp
from jax import lax
from jax.sharding import PartitionSpec as P

CZ = 128
time_step = 0.4
weno_floor = 1e-06
SPAN = 3


def exchange(fields, axis, widths, dim):
    size = lax.axis_size(axis)
    up = [(i, (i + 1) % size) for i in range(size)]
    down = [(j, i) for i, j in up]
    out = []
    for field, w in zip(fields, widths):
        d = dim + field.ndim - 3
        last = lax.slice_in_dim(field, field.shape[d] - w, field.shape[d], axis=d)
        first = lax.slice_in_dim(field, 0, w, axis=d)
        before = lax.ppermute(last, axis, up)
        after = lax.ppermute(first, axis, down)
        out.append(jnp.concatenate([before, field, after], axis=d))
    return out


def exchange_packed(fields, axis, widths):
    size = lax.axis_size(axis)
    up = [(i, (i + 1) % size) for i in range(size)]
    down = [(j, i) for i, j in up]
    dims = [field.ndim - 3 for field in fields]
    lasts = [
        lax.slice_in_dim(field, field.shape[d] - w, field.shape[d], axis=d)
        for field, w, d in zip(fields, widths, dims)
    ]
    firsts = [lax.slice_in_dim(field, 0, w, axis=d) for field, w, d in zip(fields, widths, dims)]

    def pack(parts):
        return jnp.concatenate([part.reshape(-1, part.shape[-1]) for part in parts], 0)

    def unpack(flat, like):
        out, at = ([], 0)
        for part in like:
            rows = part.size // part.shape[-1]
            out.append(flat[at : at + rows].reshape(part.shape))
            at += rows
        return out

    before = unpack(lax.ppermute(pack(lasts), axis, up), lasts)
    after = unpack(lax.ppermute(pack(firsts), axis, down), firsts)
    return [
        jnp.concatenate([b, field, a], axis=d)
        for b, field, a, d in zip(before, fields, after, dims)
    ]


def z_faces(x):
    size, length = (lax.axis_size("gz"), x.shape[2])
    up = [(i, (i + 1) % size) for i in range(size)]
    down = [(j, i) for i, j in up]
    before = lax.ppermute(x[:, :, length - SPAN :], "gz", up)
    after = lax.ppermute(x[:, :, :SPAN], "gz", down)
    return jnp.concatenate([before, x, after], axis=2)


def square(operand):
    return operand * operand


def weno_value(diff_one, diff_two, diff_three, diff_four, diff_five):
    candidate_one = diff_one / 3.0 - 7.0 * diff_two / 6.0 + 11.0 * diff_three / 6.0
    candidate_two = -diff_two / 6.0 + 5.0 * diff_three / 6.0 + diff_four / 3.0
    candidate_three = diff_three / 3.0 + 5.0 * diff_four / 6.0 - diff_five / 6.0
    smooth_one = 13.0 / 12.0 * square(diff_one - 2.0 * diff_two + diff_three) + 0.25 * square(
        diff_one - 4.0 * diff_two + 3.0 * diff_three
    )
    smooth_two = 13.0 / 12.0 * square(diff_two - 2.0 * diff_three + diff_four) + 0.25 * square(
        diff_two - diff_four
    )
    smooth_three = 13.0 / 12.0 * square(diff_three - 2.0 * diff_four + diff_five) + 0.25 * square(
        3.0 * diff_three - 4.0 * diff_four + diff_five
    )
    weight_one = 0.1 / square(weno_floor + smooth_one)
    weight_two = 0.6 / square(weno_floor + smooth_two)
    weight_three = 0.3 / square(weno_floor + smooth_three)
    return (
        weight_one * candidate_one + weight_two * candidate_two + weight_three * candidate_three
    ) / (weight_one + weight_two + weight_three)


def window(padded, axis_dim, offset):
    length = padded.shape[axis_dim] - 2 * SPAN
    return lax.slice_in_dim(padded, SPAN + offset, SPAN + offset + length, axis=axis_dim)


def local_rate(padded_list, speeds):
    summed = jnp.zeros(speeds.shape[1:], jnp.float32)
    for axis_dim in range(3):
        padded = padded_list[axis_dim]
        jump_list = [
            window(padded, axis_dim, offset) - window(padded, axis_dim, offset - 1)
            for offset in range(-2, 4)
        ]
        from_left = weno_value(jump_list[0], jump_list[1], jump_list[2], jump_list[3], jump_list[4])
        from_right = weno_value(
            jump_list[5], jump_list[4], jump_list[3], jump_list[2], jump_list[1]
        )
        speed_axis = speeds[axis_dim]
        summed = (
            summed
            + jnp.maximum(speed_axis, 0.0) * from_left
            + jnp.minimum(speed_axis, 0.0) * from_right
        )
    return -summed


def shade(samples, alive, ascending):
    opacity = alive * (2.0 / CZ) / (1.0 + 4.0 * samples * samples)
    log_clear = jnp.log1p(-opacity)
    depth = jnp.arange(CZ)
    ahead = jnp.where(
        ascending, depth[:, None] < depth[None, :], depth[:, None] > depth[None, :]
    ).astype(jnp.float32)
    flat_logs = log_clear.reshape(-1, CZ)
    before = jnp.dot(flat_logs, ahead, precision=lax.Precision.HIGH).reshape(log_clear.shape)
    weight = jnp.exp(before) * opacity
    bright = jnp.tanh(samples)
    red = jnp.sum(weight * (0.5 + 0.5 * bright), -1)
    green = jnp.sum(weight * (0.5 - 0.5 * bright), -1)
    blue = jnp.sum(weight / (1.0 + samples * samples), -1)
    clear = jnp.exp(jnp.sum(log_clear, -1))
    return jnp.stack([red, green, blue, clear])


def alternate(grid_pairs):
    row_list = [jnp.stack(pixel_pair, -1) for pixel_pair in grid_pairs]
    joined = jnp.stack(row_list, -3)
    joined_shape = joined.shape
    return joined.reshape(joined_shape[:-4] + (joined_shape[-4] * 2, joined_shape[-2] * 2))


def over(front_part, back_part):
    colour = front_part[:3] + front_part[3:] * back_part[:3]
    clear = front_part[3:] * back_part[3:]
    return jnp.concatenate([colour, clear], 0)


def x_faces(x, width):
    size, length = (lax.axis_size("gx"), x.shape[0])
    up = [(i, (i + 1) % size) for i in range(size)]
    down = [(j, i) for i, j in up]
    before = lax.ppermute(x[length - width :], "gx", up)
    after = lax.ppermute(x[:width], "gx", down)
    return jnp.concatenate([before, x, after], axis=0)


def stage_rate(field, speeds):
    inner = field[:, SPAN:-SPAN]
    padded = [x_faces(inner, SPAN), field, z_faces(inner)]
    return (inner, local_rate(padded, speeds))


def shards(level_set, velocity, active_brick, depth_order):
    alive = active_brick[0, 0, 0] > 0
    alive_float = alive.astype(jnp.float32)
    flags = jnp.broadcast_to(alive_float, level_set.shape)
    stacked = jnp.stack([level_set] + [velocity[d].astype(jnp.float32) for d in range(3)] + [flags])
    halo = 3 * SPAN + 1
    stacked = exchange([stacked], "gy", [halo], 1)[0]
    level_ext = stacked[0]
    carried = stacked[1:5, :, SPAN:-SPAN]
    speed_one = carried[:3]
    speed_two = speed_one[:, :, SPAN:-SPAN]
    flag_ring = stacked[4, :, 3 * SPAN : -3 * SPAN]
    size = lax.axis_size("gx")
    up = [(i, (i + 1) % size) for i in range(size)]
    down = [(j, i) for i, j in up]
    inner = level_ext[:, SPAN:-SPAN]
    last = jnp.concatenate([inner[-SPAN:]] + [carried[c, -1:] for c in range(4)], 0)
    first = jnp.concatenate([inner[:SPAN]] + [carried[c, :1] for c in range(4)], 0)
    before = lax.ppermute(last, "gx", up)
    after = lax.ppermute(first, "gx", down)
    padded = [jnp.concatenate([before[:SPAN], inner, after[:SPAN]], 0), level_ext, z_faces(inner)]
    section_one = inner + time_step * local_rate(padded, speed_one)
    inner, rate = stage_rate(section_one, speed_two)
    section_two = 0.75 * level_ext[:, 2 * SPAN : -2 * SPAN] + 0.25 * (inner + time_step * rate)
    ring = slice(2 * SPAN, -2 * SPAN)
    edge_before = before[SPAN - 1 :, ring]
    edge_after = jnp.concatenate([after[:1], after[SPAN:]], 0)[:, ring]
    wide = x_faces(section_two, SPAN + 1)
    inner = wide[SPAN:-SPAN, SPAN:-SPAN]
    across, along, depth = (wide[:, SPAN:-SPAN], wide[SPAN:-SPAN], z_faces(inner))
    rows = inner.shape[0]

    def part(lo, hi, speeds, level, flag):
        padded = [across[lo : hi + 2 * SPAN], along[lo:hi], depth[lo:hi]]
        rate = local_rate(padded, speeds)
        advanced = level / 3.0 + 2.0 / 3.0 * (inner[lo:hi] + time_step * rate)
        return jnp.where(flag > 0, advanced, level)

    rim = jnp.concatenate(
        [
            part(0, 1, edge_before[1:4][:, None], edge_before[:1], edge_before[4:5]),
            part(
                1,
                rows - 1,
                speed_two[:, :, SPAN:-SPAN],
                level_ext[:, 3 * SPAN : -3 * SPAN],
                flag_ring,
            ),
            part(rows - 1, rows, edge_after[1:4][:, None], edge_after[:1], edge_after[4:5]),
        ],
        0,
    )
    level_out = rim[1:-1, 1:-1]
    group = lax.axis_size("gz")
    ascending = depth_order[0] < depth_order[group - 1]
    left_x = 0.75 * rim[1:-1] + 0.25 * rim[:-2]
    right_x = 0.75 * rim[1:-1] + 0.25 * rim[2:]
    grid_pairs = []
    for along_x in (left_x, right_x):
        pair_list = []
        for neighbour in (along_x[:, :-2], along_x[:, 2:]):
            samples = 0.75 * along_x[:, 1:-1] + 0.25 * neighbour
            pair_list.append(shade(samples, alive_float, ascending))
        grid_pairs.append(pair_list)
    slab_image = alternate(grid_pairs)
    rows_each = slab_image.shape[1] // group
    columns = slab_image.shape[2]
    pieces = slab_image.reshape(4, group, rows_each, columns)
    received = lax.all_to_all(pieces, "gz", split_axis=1, concat_axis=1, tiled=True)
    blended = jnp.concatenate(
        [
            jnp.zeros((3, rows_each, columns), jnp.float32),
            jnp.ones((1, rows_each, columns), jnp.float32),
        ],
        0,
    )
    for rank_value in range(group):
        chooser = (depth_order == rank_value).astype(jnp.float32)
        piece_now = jnp.einsum("s,csij->cij", chooser, received, precision=lax.Precision.HIGHEST)
        blended = over(blended, piece_now)
    image = jnp.concatenate([blended[:3], 1.0 - blended[3:]], 0)
    return (level_out, image)


def solution(mesh):
    placed = (P("gx", "gy", "gz"), P(None, "gx", "gy", "gz"), P("gx", "gy", "gz"), P())
    return jax.shard_map(
        shards,
        mesh=mesh,
        in_specs=placed,
        out_specs=(P("gx", "gy", "gz"), P(None, ("gx", "gz"), "gy")),
        check_vma=False,
    )
```

profile of v0, /device:TPU:135, one launch (start us, length us, event | category | flops | bytes accessed | tf_op | source)
XLA Modules:
  0.0 186.2 jit_solution(2061402217357418076)
XLA Ops:
  4.1 4.6 %collective-permute-start.1 = (f32[5,32,10,128]{3,1,2,0:T(8,128)S(1)}, f32[5,32,10,128]{3,1,2,0:T(8,128)S(1)}, u32[]{:S(2)}, u32[]{:S(2)}) collective-permute-start(f32[5,32,10,128]{3,1,2,0:T(8,128)S(1)} %copy.8), channel_id=1, source_target_pairs={{4,0},{8,4},{12,8},{0,12},{5,1},{9,5},{13,9},{1,13},{6,2},{10,6},{... | collective-permute-start | bytes 2457608 | tf_op jit(solution)/shard_map/ppermute | solution.py:22
  9.0 1.9 %collective-permute-start = (f32[5,32,10,128]{3,1,2,0:T(8,128)S(1)}, f32[5,32,10,128]{3,1,2,0:T(8,128)S(1)}, u32[]{:S(2)}, u32[]{:S(2)}) collective-permute-start(f32[5,32,10,128]{3,1,2,0:T(8,128)S(1)} %copy.7), channel_id=1, source_target_pairs={{0,4},{4,8},{8,12},{12,0},{1,5},{5,9},{9,13},{13,1},{2,6},{6,10},{... | collective-permute-start | bytes 2457608 | tf_op jit(solution)/shard_map/ppermute | solution.py:21
  11.0 14.7 %collective-permute-done.1 = f32[5,32,10,128]{3,1,2,0:T(8,128)S(1)} collective-permute-done((f32[5,32,10,128]{3,1,2,0:T(8,128)S(1)}, f32[5,32,10,128]{3,1,2,0:T(8,128)S(1)}, u32[]{:S(2)}, u32[]{:S(2)}) %collective-permute-start.1) | collective-permute-done | bytes 819232 | tf_op jit(solution)/shard_map/ppermute | solution.py:22
  26.2 4.8 %collective-permute-done = f32[5,32,10,128]{3,1,2,0:T(8,128)S(1)} collective-permute-done((f32[5,32,10,128]{3,1,2,0:T(8,128)S(1)}, f32[5,32,10,128]{3,1,2,0:T(8,128)S(1)}, u32[]{:S(2)}, u32[]{:S(2)}) %collective-permute-start) | collective-permute-done | bytes 819232 | tf_op jit(solution)/shard_map/ppermute | solution.py:21
  32.9 1.1 constant_dynamic-update-slice_fusion.7
  36.0 10.4 %collective-permute-start.2 = (f32[7,46,128]{2,1,0:T(8,128)}, f32[7,46,128]{2,1,0:T(8,128)S(1)}, u32[]{:S(2)}, u32[]{:S(2)}) collective-permute-start(f32[7,46,128]{2,1,0:T(8,128)} %get-tuple-element.19), channel_id=1, source_target_pairs={{0,16},{16,32},{32,48},{48,64},{64,80},{80,96},{96,112},{112,128},... | collective-permute-start | bytes 494600 | tf_op jit(solution)/shard_map/ppermute | solution.py:181
  46.4 1.9 %collective-permute-start.3 = (f32[7,46,128]{2,1,0:T(8,128)}, f32[7,46,128]{2,1,0:T(8,128)}, u32[]{:S(2)}, u32[]{:S(2)}) collective-permute-start(f32[7,46,128]{2,1,0:T(8,128)} %get-tuple-element.18), channel_id=1, source_target_pairs={{16,0},{32,16},{48,32},{64,48},{80,64},{96,80},{112,96},{128,112},... | collective-permute-start | bytes 494600 | tf_op jit(solution)/shard_map/ppermute | solution.py:182
  49.0 2.6 %collective-permute-start.4 = (f32[32,46,3]{1,0,2:T(8,128)S(1)}, f32[32,46,3]{1,0,2:T(8,128)S(1)}, u32[]{:S(2)}, u32[]{:S(2)}) collective-permute-start(f32[32,46,3]{1,0,2:T(8,128)S(1)} %copy.11), channel_id=1, source_target_pairs={{0,1},{1,2},{2,3},{3,0},{4,5},{5,6},{6,7},{7,4},{8,9},{9,10},{10,1... | collective-permute-start | bytes 53000 | tf_op jit(solution)/shard_map/ppermute | solution.py:61
  52.0 4.4 %collective-permute-start.5 = (f32[32,46,3]{1,0,2:T(8,128)S(1)}, f32[32,46,3]{1,0,2:T(8,128)S(1)}, u32[]{:S(2)}, u32[]{:S(2)}) collective-permute-start(f32[32,46,3]{1,0,2:T(8,128)S(1)} %copy.13), channel_id=1, source_target_pairs={{1,0},{2,1},{3,2},{0,3},{5,4},{6,5},{7,6},{4,7},{9,8},{10,9},{11,1... | collective-permute-start | bytes 53000 | tf_op jit(solution)/shard_map/ppermute | solution.py:62
  56.5 1.3 copy.12
  57.8 1.3 copy.14
  59.1 3.0 %collective-permute-done.3 = f32[7,46,128]{2,1,0:T(8,128)} collective-permute-done((f32[7,46,128]{2,1,0:T(8,128)}, f32[7,46,128]{2,1,0:T(8,128)}, u32[]{:S(2)}, u32[]{:S(2)}) %collective-permute-start.3) | collective-permute-done | bytes 164896 | tf_op jit(solution)/shard_map/ppermute | solution.py:182
  63.0 15.0 %fusion.21 = f32[32,46,128]{2,1,0:T(8,128)S(1)} fusion(f32[32,46,128]{2,1,0:T(8,128)S(1)} %slice.976, f32[32,46,3]{2,1,0:T(8,128)} %copy.14, f32[32,46,3]{2,1,0:T(8,128)} %copy.12, f32[5,32,52,128]{3,2,1,0:T(8,128)} %copy-done, f32[32,52,128]{2,1,0:T(8,128)S(1)} %slice_bitcast_fusion, f32[3,46,128]{2,1,0:T(8,128)S(1)} %slice.979, f32[3,46,128]{2,1,0:T(8,128)S(1)} %slice.985), kind=kLoop, calls=%fused_computation.99 | loop fusion | flops 79511552 | bytes 8466944 | tf_op jit(solution)/shard_map/add | solution.py:184
  78.0 10.1 %collective-permute-start.6 = (f32[3,40,128]{2,1,0:T(8,128)S(1)}, f32[3,40,128]{2,1,0:T(8,128)S(1)}, u32[]{:S(2)}, u32[]{:S(2)}) collective-permute-start(f32[3,40,128]{2,1,0:T(8,128)S(1)} %get-tuple-element.35), channel_id=1, source_target_pairs={{0,16},{16,32},{32,48},{48,64},{64,80},{80,96},{96,112},{112,128},... | collective-permute-start | bytes 184328 | tf_op jit(solution)/shard_map/ppermute | solution.py:152
  88.2 1.9 %collective-permute-start.7 = (f32[3,40,128]{2,1,0:T(8,128)S(1)}, f32[3,40,128]{2,1,0:T(8,128)S(1)}, u32[]{:S(2)}, u32[]{:S(2)}) collective-permute-start(f32[3,40,128]{2,1,0:T(8,128)S(1)} %get-tuple-element.34), channel_id=1, source_target_pairs={{16,0},{32,16},{48,32},{64,48},{80,64},{96,80},{112,96},{128,112},... | collective-permute-start | bytes 184328 | tf_op jit(solution)/shard_map/ppermute | solution.py:153
  90.6 1.9 %collective-permute-start.8 = (f32[32,40,3]{1,0,2:T(8,128)S(1)}, f32[32,40,3]{1,0,2:T(8,128)S(1)}, u32[]{:S(2)}, u32[]{:S(2)}) collective-permute-start(f32[32,40,3]{1,0,2:T(8,128)S(1)} %copy.15), channel_id=1, source_target_pairs={{0,1},{1,2},{2,3},{3,0},{4,5},{5,6},{6,7},{7,4},{8,9},{9,10},{10,1... | collective-permute-start | bytes 46088 | tf_op jit(solution)/shard_map/ppermute | solution.py:61
  93.5 5.1 %collective-permute-start.9 = (f32[32,40,3]{1,0,2:T(8,128)}, f32[32,40,3]{1,0,2:T(8,128)S(1)}, u32[]{:S(2)}, u32[]{:S(2)}) collective-permute-start(f32[32,40,3]{1,0,2:T(8,128)} %copy.17), channel_id=1, source_target_pairs={{1,0},{2,1},{3,2},{0,3},{5,4},{6,5},{7,6},{4,7},{9,8},{10,9},{11,1... | collective-permute-start | bytes 46088 | tf_op jit(solution)/shard_map/ppermute | solution.py:62
  98.7 1.2 copy.16
  100.1 1.2 copy.18
  101.3 13.0 %fusion.174 = f32[32,40,128]{2,1,0:T(8,128)S(1)} fusion(f32[32,52,128]{2,1,0:T(8,128)S(1)} %slice_bitcast_fusion, f32[32,40,128]{2,1,0:T(8,128)S(1)} %slice.1008, f32[32,40,3]{2,1,0:T(8,128)} %copy.18, f32[32,40,3]{2,1,0:T(8,128)} %copy.16, f32[5,32,52,128]{3,2,1,0:T(8,128)} %copy-done, f32[32,46,128]{2,1,0:T(8,128)S(1)} %fusion.21, ...), kind=kLoop, calls=%fused_computation.299 | loop fusion | flops 69632000 | bytes 8017920 | tf_op jit(solution)/shard_map/add | solution.py:186
  114.3 10.8 %collective-permute-start.10 = (f32[4,40,128]{2,1,0:T(8,128)S(1)}, f32[4,40,128]{2,1,0:T(8,128)S(1)}, u32[]{:S(2)}, u32[]{:S(2)}) collective-permute-start(f32[4,40,128]{2,1,0:T(8,128)S(1)} %get-tuple-element.44), channel_id=1, source_target_pairs={{0,16},{16,32},{32,48},{48,64},{64,80},{80,96},{96,112},{112,128},... | collective-permute-start | bytes 245768 | tf_op jit(solution)/shard_map/ppermute | solution.py:152
  125.1 1.9 %collective-permute-start.11 = (f32[4,40,128]{2,1,0:T(8,128)S(1)}, f32[4,40,128]{2,1,0:T(8,128)S(1)}, u32[]{:S(2)}, u32[]{:S(2)}) collective-permute-start(f32[4,40,128]{2,1,0:T(8,128)S(1)} %get-tuple-element.45), channel_id=1, source_target_pairs={{16,0},{32,16},{48,32},{64,48},{80,64},{96,80},{112,96},{128,112},... | collective-permute-start | bytes 245768 | tf_op jit(solution)/shard_map/ppermute | solution.py:153
  127.2 10.0 %collective-permute-done.11 = f32[4,40,128]{2,1,0:T(8,128)S(1)} collective-permute-done((f32[4,40,128]{2,1,0:T(8,128)S(1)}, f32[4,40,128]{2,1,0:T(8,128)S(1)}, u32[]{:S(2)}, u32[]{:S(2)}) %collective-permute-start.11) | collective-permute-done | bytes 81952 | tf_op jit(solution)/shard_map/ppermute | solution.py:153
  137.2 1.1 fusion.456
  138.3 1.5 copy.19
  139.8 1.9 %collective-permute-start.12 = (f32[34,34,3]{1,0,2:T(8,128)S(1)}, f32[34,34,3]{1,0,2:T(8,128)S(1)}, u32[]{:S(2)}, u32[]{:S(2)}) collective-permute-start(f32[34,34,3]{1,0,2:T(8,128)S(1)} %copy.19), channel_id=1, source_target_pairs={{0,1},{1,2},{2,3},{3,0},{4,5},{5,6},{6,7},{7,4},{8,9},{9,10},{10,1... | collective-permute-start | bytes 41624 | tf_op jit(solution)/shard_map/ppermute | solution.py:61
  142.7 5.8 %collective-permute-start.13 = (f32[34,34,3]{1,0,2:T(8,128)}, f32[34,34,3]{1,0,2:T(8,128)S(1)}, u32[]{:S(2)}, u32[]{:S(2)}) collective-permute-start(f32[34,34,3]{1,0,2:T(8,128)} %copy.21), channel_id=1, source_target_pairs={{1,0},{2,1},{3,2},{0,3},{5,4},{6,5},{7,6},{4,7},{9,8},{10,9},{11,1... | collective-permute-start | bytes 41624 | tf_op jit(solution)/shard_map/ppermute | solution.py:62
  152.0 1.5 add_select_fusion
  153.8 13.2 %fusion.181 = f32[32,34,128]{2,1,0:T(8,128)S(1)} fusion(f32[34,34,3]{2,1,0:T(8,128)S(1)} %copy.22, f32[34,34,128]{2,1,0:T(8,128)S(1)} %copy-done.1, f32[34,34,3]{2,1,0:T(8,128)S(1)} %copy.20, f32[5,32,52,128]{3,2,1,0:T(8,128)} %copy-done, f32[32,40,128]{2,1,0:T(8,128)S(1)} %fusion.174, f32[4,40,128]{2,1,0:T(8,128)S(1)} %collective-permute-done.11, ...), kind=kLoop, calls=%fused_computation.308 | loop fusion | flops 59465728 | bytes 10936320 | tf_op jit(solution)/shard_map/jit(_where)/select_n | solution.py:199
  172.2 1.3 copy.23
  175.0 3.3 %all-to-all-start = ((f32[4,1,4096]{2,1,0:T(1,128)}), f32[4,1,4096]{2,1,0:T(1,128)S(1)}, u32[]{:S(2)}, u32[]{:S(2)}) async-start(f32[4,1,4096]{2,1,0:T(1,128)} %reshape.120), calls=%async_computation | async-start | bytes 131072 | tf_op jit(solution)/shard_map/all_to_all | solution.py:231
  179.1 3.7 %all-to-all-done = f32[4,1,4096]{2,1,0:T(1,128)S(1)} async-done(((f32[4,1,4096]{2,1,0:T(1,128)}), f32[4,1,4096]{2,1,0:T(1,128)S(1)}, u32[]{:S(2)}, u32[]{:S(2)}) %all-to-all-start) | async-done | bytes 65568 | tf_op jit(solution)/shard_map/all_to_all | solution.py:231
  (87 shorter events, 25.5 us)
Async XLA Ops:
  0.6 2.8 %copy-start.4 = (bf16[3,32,32,128]{3,2,1,0:T(8,128)(2,1)S(1)}, bf16[3,32,32,128]{3,2,1,0:T(8,128)(2,1)}, u32[]{:S(2)}) copy-start(bf16[3,32,32,128]{3,2,1,0:T(8,128)(2,1)} %param.5) | copy-start | bytes 2359300
  4.1 21.6 %collective-permute-start.1 = (f32[5,32,10,128]{3,1,2,0:T(8,128)S(1)}, f32[5,32,10,128]{3,1,2,0:T(8,128)S(1)}, u32[]{:S(2)}, u32[]{:S(2)}) collective-permute-start(f32[5,32,10,128]{3,1,2,0:T(8,128)S(1)} %copy.8), channel_id=1, source_target_pairs={{4,0},{8,4},{12,8},{0,12},{5,1},{9,5},{13,9},{1,13},{6,2},{10,6},{... | collective-permute-start | bytes 2457608 | tf_op jit(solution)/shard_map/ppermute | solution.py:22
  9.0 22.0 %collective-permute-start = (f32[5,32,10,128]{3,1,2,0:T(8,128)S(1)}, f32[5,32,10,128]{3,1,2,0:T(8,128)S(1)}, u32[]{:S(2)}, u32[]{:S(2)}) collective-permute-start(f32[5,32,10,128]{3,1,2,0:T(8,128)S(1)} %copy.7), channel_id=1, source_target_pairs={{0,4},{4,8},{8,12},{12,0},{1,5},{5,9},{9,13},{13,1},{2,6},{6,10},{... | collective-permute-start | bytes 2457608 | tf_op jit(solution)/shard_map/ppermute | solution.py:21
  32.0 2.1 %copy-start = (f32[5,32,52,128]{3,2,1,0:T(8,128)}, f32[5,32,52,128]{3,2,1,0:T(8,128)S(1)}, u32[]{:S(2)}) copy-start(f32[5,32,52,128]{3,2,1,0:T(8,128)S(1)} %pad_maximum_fusion) | copy-start | bytes 12779524
  36.0 23.0 %collective-permute-start.2 = (f32[7,46,128]{2,1,0:T(8,128)}, f32[7,46,128]{2,1,0:T(8,128)S(1)}, u32[]{:S(2)}, u32[]{:S(2)}) collective-permute-start(f32[7,46,128]{2,1,0:T(8,128)} %get-tuple-element.19), channel_id=1, source_target_pairs={{0,16},{16,32},{32,48},{48,64},{64,80},{80,96},{96,112},{112,128},... | collective-permute-start | bytes 494600 | tf_op jit(solution)/shard_map/ppermute | solution.py:181
  46.4 15.7 %collective-permute-start.3 = (f32[7,46,128]{2,1,0:T(8,128)}, f32[7,46,128]{2,1,0:T(8,128)}, u32[]{:S(2)}, u32[]{:S(2)}) collective-permute-start(f32[7,46,128]{2,1,0:T(8,128)} %get-tuple-element.18), channel_id=1, source_target_pairs={{16,0},{32,16},{48,32},{64,48},{80,64},{96,80},{112,96},{128,112},... | collective-permute-start | bytes 494600 | tf_op jit(solution)/shard_map/ppermute | solution.py:182
  49.0 7.5 %collective-permute-start.4 = (f32[32,46,3]{1,0,2:T(8,128)S(1)}, f32[32,46,3]{1,0,2:T(8,128)S(1)}, u32[]{:S(2)}, u32[]{:S(2)}) collective-permute-start(f32[32,46,3]{1,0,2:T(8,128)S(1)} %copy.11), channel_id=1, source_target_pairs={{0,1},{1,2},{2,3},{3,0},{4,5},{5,6},{6,7},{7,4},{8,9},{9,10},{10,1... | collective-permute-start | bytes 53000 | tf_op jit(solution)/shard_map/ppermute | solution.py:61
  52.0 5.8 %collective-permute-start.5 = (f32[32,46,3]{1,0,2:T(8,128)S(1)}, f32[32,46,3]{1,0,2:T(8,128)S(1)}, u32[]{:S(2)}, u32[]{:S(2)}) collective-permute-start(f32[32,46,3]{1,0,2:T(8,128)S(1)} %copy.13), channel_id=1, source_target_pairs={{1,0},{2,1},{3,2},{0,3},{5,4},{6,5},{7,6},{4,7},{9,8},{10,9},{11,1... | collective-permute-start | bytes 53000 | tf_op jit(solution)/shard_map/ppermute | solution.py:62
  78.0 23.2 %collective-permute-start.6 = (f32[3,40,128]{2,1,0:T(8,128)S(1)}, f32[3,40,128]{2,1,0:T(8,128)S(1)}, u32[]{:S(2)}, u32[]{:S(2)}) collective-permute-start(f32[3,40,128]{2,1,0:T(8,128)S(1)} %get-tuple-element.35), channel_id=1, source_target_pairs={{0,16},{16,32},{32,48},{48,64},{64,80},{80,96},{96,112},{112,128},... | collective-permute-start | bytes 184328 | tf_op jit(solution)/shard_map/ppermute | solution.py:152
  88.2 13.1 %collective-permute-start.7 = (f32[3,40,128]{2,1,0:T(8,128)S(1)}, f32[3,40,128]{2,1,0:T(8,128)S(1)}, u32[]{:S(2)}, u32[]{:S(2)}) collective-permute-start(f32[3,40,128]{2,1,0:T(8,128)S(1)} %get-tuple-element.34), channel_id=1, source_target_pairs={{16,0},{32,16},{48,32},{64,48},{80,64},{96,80},{112,96},{128,112},... | collective-permute-start | bytes 184328 | tf_op jit(solution)/shard_map/ppermute | solution.py:153
  90.6 8.1 %collective-permute-start.8 = (f32[32,40,3]{1,0,2:T(8,128)S(1)}, f32[32,40,3]{1,0,2:T(8,128)S(1)}, u32[]{:S(2)}, u32[]{:S(2)}) collective-permute-start(f32[32,40,3]{1,0,2:T(8,128)S(1)} %copy.15), channel_id=1, source_target_pairs={{0,1},{1,2},{2,3},{3,0},{4,5},{5,6},{6,7},{7,4},{8,9},{9,10},{10,1... | collective-permute-start | bytes 46088 | tf_op jit(solution)/shard_map/ppermute | solution.py:61
  93.5 6.6 %collective-permute-start.9 = (f32[32,40,3]{1,0,2:T(8,128)}, f32[32,40,3]{1,0,2:T(8,128)S(1)}, u32[]{:S(2)}, u32[]{:S(2)}) collective-permute-start(f32[32,40,3]{1,0,2:T(8,128)} %copy.17), channel_id=1, source_target_pairs={{1,0},{2,1},{3,2},{0,3},{5,4},{6,5},{7,6},{4,7},{9,8},{10,9},{11,1... | collective-permute-start | bytes 46088 | tf_op jit(solution)/shard_map/ppermute | solution.py:62
  114.3 12.8 %collective-permute-start.10 = (f32[4,40,128]{2,1,0:T(8,128)S(1)}, f32[4,40,128]{2,1,0:T(8,128)S(1)}, u32[]{:S(2)}, u32[]{:S(2)}) collective-permute-start(f32[4,40,128]{2,1,0:T(8,128)S(1)} %get-tuple-element.44), channel_id=1, source_target_pairs={{0,16},{16,32},{32,48},{48,64},{64,80},{80,96},{96,112},{112,128},... | collective-permute-start | bytes 245768 | tf_op jit(solution)/shard_map/ppermute | solution.py:152
  125.1 12.0 %collective-permute-start.11 = (f32[4,40,128]{2,1,0:T(8,128)S(1)}, f32[4,40,128]{2,1,0:T(8,128)S(1)}, u32[]{:S(2)}, u32[]{:S(2)}) collective-permute-start(f32[4,40,128]{2,1,0:T(8,128)S(1)} %get-tuple-element.45), channel_id=1, source_target_pairs={{16,0},{32,16},{48,32},{64,48},{80,64},{96,80},{112,96},{128,112},... | collective-permute-start | bytes 245768 | tf_op jit(solution)/shard_map/ppermute | solution.py:153
  137.2 11.3 %copy-start.5 = (s32[4]{0:T(128)S(1)}, s32[4]{0:T(128)}, u32[]{:S(2)}) copy-start(s32[4]{0:T(128)} %param.7) | copy-start | bytes 52
  139.8 11.5 %collective-permute-start.12 = (f32[34,34,3]{1,0,2:T(8,128)S(1)}, f32[34,34,3]{1,0,2:T(8,128)S(1)}, u32[]{:S(2)}, u32[]{:S(2)}) collective-permute-start(f32[34,34,3]{1,0,2:T(8,128)S(1)} %copy.19), channel_id=1, source_target_pairs={{0,1},{1,2},{2,3},{3,0},{4,5},{5,6},{6,7},{7,4},{8,9},{9,10},{10,1... | collective-permute-start | bytes 41624 | tf_op jit(solution)/shard_map/ppermute | solution.py:61
  142.7 8.9 %collective-permute-start.13 = (f32[34,34,3]{1,0,2:T(8,128)}, f32[34,34,3]{1,0,2:T(8,128)S(1)}, u32[]{:S(2)}, u32[]{:S(2)}) collective-permute-start(f32[34,34,3]{1,0,2:T(8,128)} %copy.21), channel_id=1, source_target_pairs={{1,0},{2,1},{3,2},{0,3},{5,4},{6,5},{7,6},{4,7},{9,8},{10,9},{11,1... | collective-permute-start | bytes 41624 | tf_op jit(solution)/shard_map/ppermute | solution.py:62
  152.0 1.5 copy-start.1
  167.1 0.8 copy-start.2
  173.5 4.7 %copy-start.3 = (f32[32,34,128]{2,1,0:T(8,128)S(1)}, f32[32,34,128]{2,1,0:T(8,128)}, u32[]{:S(2)}) copy-start(f32[32,34,128]{2,1,0:T(8,128)} %copy-done.2) | copy-start | bytes 1671172
  175.0 7.9 %all-to-all-start = ((f32[4,1,4096]{2,1,0:T(1,128)}), f32[4,1,4096]{2,1,0:T(1,128)S(1)}, u32[]{:S(2)}, u32[]{:S(2)}) async-start(f32[4,1,4096]{2,1,0:T(1,128)} %reshape.120), calls=%async_computation | async-start | bytes 131072 | tf_op jit(solution)/shard_map/all_to_all | solution.py:231
where the time goes:
time: 187 us; the launch traced here: 186 us
  starting transfers between devices  68.8 us (37%)
  other arithmetic  49.7 us (27%)
  waiting for transfers between devices  36.6 us (20%)
  local copies, waits for them, and re-layouts  22.6 us (12%)
  matrix products  5.36 us (3%)
  between operations  3.14 us (2%)
    ppermute x2, starting transfers between devices, x_faces(): before = lax.ppermute(x[length - width:], 'gx', up)  20.9 us
    ppermute x3, starting transfers between devices, z_faces(): after = lax.ppermute(x[:, :, :SPAN], 'gz', down)  15.4 us
    select_n x3, other arithmetic, part(): return jnp.where(flag > 0, advanced, level)  15.1 us
    add x1, other arithmetic, shards(): section_one = inner + time_step * local_rate(padded, speed_one)  15 us
    ppermute x1, waiting for transfers between devices, exchange(): after = lax.ppermute(first, axis, down)  14.7 us
    add x1, other arithmetic, shards(): 0.75 * level_ext[:, 2 * SPAN:-2 * SPAN] + 0.25 * (inner + time_step * rate)  13 us
    ppermute x1, starting transfers between devices, shards(): before = lax.ppermute(last, 'gx', up)  10.4 us
    ppermute x2, waiting for transfers between devices, x_faces(): after = lax.ppermute(x[:width], 'gx', down)  9.96 us
  transfers between devices with their start and end apart: 15, of which 7 were waited for; matrix products, arithmetic and copies ran while one was open for 6% of the time, Pallas kernels for 0%

commit v1 on v0

--- a/solution.py
+++ b/solution.py
@@ -7,6 +7,13 @@
 time_step = 0.4
 weno_floor = 1e-06
 SPAN = 3
+
+
+def swap_blocks(x, axis, split, join):
+    devices = lax.axis_size(axis)
+    blocks = jnp.stack(jnp.split(x, devices, axis=split), axis=0)
+    blocks = lax.all_to_all(blocks, axis, split_axis=0, concat_axis=0)
+    return jnp.concatenate(blocks, axis=join)
 
 
 def exchange(fields, axis, widths, dim):
@@ -228,7 +235,7 @@
     rows_each = slab_image.shape[1] // group
     columns = slab_image.shape[2]
     pieces = slab_image.reshape(4, group, rows_each, columns)
-    received = lax.all_to_all(pieces, "gz", split_axis=1, concat_axis=1, tiled=True)
+    received = swap_blocks(pieces, "gz", 1, 1)
     blended = jnp.concatenate(
         [
             jnp.zeros((3, rows_each, columns), jnp.float32),

time: 187 us -> 188 us (level)
  the two profiles are of different devices: /device:TPU:135 before, /device:TPU:143 now
where the time goes in v1:
time: 188 us; the launch traced here: 187 us
  starting transfers between devices  67.6 us (36%)
  other arithmetic  49.8 us (26%)
  waiting for transfers between devices  35.2 us (19%)
  local copies, waits for them, and re-layouts  26 us (14%)
  matrix products  5.36 us (3%)
  between operations  3.15 us (2%)
    ppermute x2, starting transfers between devices, x_faces(): before = lax.ppermute(x[length - width:], 'gx', up)  20.9 us
    ppermute x1, waiting for transfers between devices, exchange(): before = lax.ppermute(last, axis, up)  15.5 us
    ppermute x3, starting transfers between devices, z_faces(): after = lax.ppermute(x[:, :, :SPAN], 'gz', down)  15.4 us
    select_n x3, other arithmetic, part(): return jnp.where(flag > 0, advanced, level)  15.1 us
    add x1, other arithmetic, shards(): section_one = inner + time_step * local_rate(padded, speed_one)  15 us
    add x1, other arithmetic, shards(): 0.75 * level_ext[:, 2 * SPAN:-2 * SPAN] + 0.25 * (inner + time_step * rate)  13 us
    ppermute x1, starting transfers between devices, shards(): before = lax.ppermute(last, 'gx', up)  10.4 us
    ppermute x2, waiting for transfers between devices, x_faces(): after = lax.ppermute(x[:width], 'gx', down)  9.96 us
  transfers between devices with their start and end apart: 15, of which 7 were waited for; matrix products, arithmetic and copies ran while one was open for 6% of the time, Pallas kernels for 0%

profile of v1, /device:TPU:143, one launch (start us, length us, event | category | flops | bytes accessed | tf_op | source)
XLA Modules:
  0.0 187.1 jit_solution(18389613495031028751)
XLA Ops:
  4.1 3.2 %collective-permute-start = (f32[5,32,10,128]{3,1,2,0:T(8,128)S(1)}, f32[5,32,10,128]{3,1,2,0:T(8,128)S(1)}, u32[]{:S(2)}, u32[]{:S(2)}) collective-permute-start(f32[5,32,10,128]{3,1,2,0:T(8,128)S(1)} %copy.10), channel_id=1, source_target_pairs={{0,4},{4,8},{8,12},{12,0},{1,5},{5,9},{9,13},{13,1},{2,6},{6,10},{... | collective-permute-start | bytes 2457608 | tf_op jit(solution)/shard_map/ppermute | solution.py:28
  7.6 2.1 %collective-permute-start.1 = (f32[5,32,10,128]{3,1,2,0:T(8,128)S(1)}, f32[5,32,10,128]{3,1,2,0:T(8,128)S(1)}, u32[]{:S(2)}, u32[]{:S(2)}) collective-permute-start(f32[5,32,10,128]{3,1,2,0:T(8,128)S(1)} %copy.11), channel_id=1, source_target_pairs={{4,0},{8,4},{12,8},{0,12},{5,1},{9,5},{13,9},{1,13},{6,2},{10,6},{... | collective-permute-start | bytes 2457608 | tf_op jit(solution)/shard_map/ppermute | solution.py:29
  9.7 15.5 %collective-permute-done = f32[5,32,10,128]{3,1,2,0:T(8,128)S(1)} collective-permute-done((f32[5,32,10,128]{3,1,2,0:T(8,128)S(1)}, f32[5,32,10,128]{3,1,2,0:T(8,128)S(1)}, u32[]{:S(2)}, u32[]{:S(2)}) %collective-permute-start) | collective-permute-done | bytes 819232 | tf_op jit(solution)/shard_map/ppermute | solution.py:28
  25.6 2.7 %collective-permute-done.1 = f32[5,32,10,128]{3,1,2,0:T(8,128)S(1)} collective-permute-done((f32[5,32,10,128]{3,1,2,0:T(8,128)S(1)}, f32[5,32,10,128]{3,1,2,0:T(8,128)S(1)}, u32[]{:S(2)}, u32[]{:S(2)}) %collective-permute-start.1) | collective-permute-done | bytes 819232 | tf_op jit(solution)/shard_map/ppermute | solution.py:29
  33.4 10.4 %collective-permute-start.2 = (f32[7,46,128]{2,1,0:T(8,128)}, f32[7,46,128]{2,1,0:T(8,128)S(1)}, u32[]{:S(2)}, u32[]{:S(2)}) collective-permute-start(f32[7,46,128]{2,1,0:T(8,128)} %get-tuple-element.19), channel_id=1, source_target_pairs={{0,16},{16,32},{32,48},{48,64},{64,80},{80,96},{96,112},{112,128},... | collective-permute-start | bytes 494600 | tf_op jit(solution)/shard_map/ppermute | solution.py:188
  43.8 1.9 %collective-permute-start.3 = (f32[7,46,128]{2,1,0:T(8,128)}, f32[7,46,128]{2,1,0:T(8,128)}, u32[]{:S(2)}, u32[]{:S(2)}) collective-permute-start(f32[7,46,128]{2,1,0:T(8,128)} %get-tuple-element.18), channel_id=1, source_target_pairs={{16,0},{32,16},{48,32},{64,48},{80,64},{96,80},{112,96},{128,112},... | collective-permute-start | bytes 494600 | tf_op jit(solution)/shard_map/ppermute | solution.py:189
  46.4 2.6 %collective-permute-start.4 = (f32[32,46,3]{1,0,2:T(8,128)S(1)}, f32[32,46,3]{1,0,2:T(8,128)S(1)}, u32[]{:S(2)}, u32[]{:S(2)}) collective-permute-start(f32[32,46,3]{1,0,2:T(8,128)S(1)} %copy.14), channel_id=1, source_target_pairs={{0,1},{1,2},{2,3},{3,0},{4,5},{5,6},{6,7},{7,4},{8,9},{9,10},{10,1... | collective-permute-start | bytes 53000 | tf_op jit(solution)/shard_map/ppermute | solution.py:68
  49.4 4.4 %collective-permute-start.5 = (f32[32,46,3]{1,0,2:T(8,128)S(1)}, f32[32,46,3]{1,0,2:T(8,128)S(1)}, u32[]{:S(2)}, u32[]{:S(2)}) collective-permute-start(f32[32,46,3]{1,0,2:T(8,128)S(1)} %copy.16), channel_id=1, source_target_pairs={{1,0},{2,1},{3,2},{0,3},{5,4},{6,5},{7,6},{4,7},{9,8},{10,9},{11,1... | collective-permute-start | bytes 53000 | tf_op jit(solution)/shard_map/ppermute | solution.py:69
  53.9 1.3 copy.15
  55.2 1.3 copy.17
  56.4 3.0 %collective-permute-done.3 = f32[7,46,128]{2,1,0:T(8,128)} collective-permute-done((f32[7,46,128]{2,1,0:T(8,128)}, f32[7,46,128]{2,1,0:T(8,128)}, u32[]{:S(2)}, u32[]{:S(2)}) %collective-permute-start.3) | collective-permute-done | bytes 164896 | tf_op jit(solution)/shard_map/ppermute | solution.py:189
  60.4 15.0 %fusion.21 = f32[32,46,128]{2,1,0:T(8,128)S(1)} fusion(f32[32,46,128]{2,1,0:T(8,128)S(1)} %slice.976, f32[32,46,3]{2,1,0:T(8,128)} %copy.17, f32[32,46,3]{2,1,0:T(8,128)} %copy.15, f32[5,32,52,128]{3,2,1,0:T(8,128)} %copy-done, f32[32,52,128]{2,1,0:T(8,128)S(1)} %slice_bitcast_fusion, f32[3,46,128]{2,1,0:T(8,128)S(1)} %slice.979, f32[3,46,128]{2,1,0:T(8,128)S(1)} %slice.985), kind=kLoop, calls=%fused_computation.99 | loop fusion | flops 79511552 | bytes 8466944 | tf_op jit(solution)/shard_map/add | solution.py:191
  75.4 10.1 %collective-permute-start.6 = (f32[3,40,128]{2,1,0:T(8,128)S(1)}, f32[3,40,128]{2,1,0:T(8,128)S(1)}, u32[]{:S(2)}, u32[]{:S(2)}) collective-permute-start(f32[3,40,128]{2,1,0:T(8,128)S(1)} %get-tuple-element.39), channel_id=1, source_target_pairs={{0,16},{16,32},{32,48},{48,64},{64,80},{80,96},{96,112},{112,128},... | collective-permute-start | bytes 184328 | tf_op jit(solution)/shard_map/ppermute | solution.py:159
  85.5 1.9 %collective-permute-start.7 = (f32[3,40,128]{2,1,0:T(8,128)S(1)}, f32[3,40,128]{2,1,0:T(8,128)S(1)}, u32[]{:S(2)}, u32[]{:S(2)}) collective-permute-start(f32[3,40,128]{2,1,0:T(8,128)S(1)} %get-tuple-element.38), channel_id=1, source_target_pairs={{16,0},{32,16},{48,32},{64,48},{80,64},{96,80},{112,96},{128,112},... | collective-permute-start | bytes 184328 | tf_op jit(solution)/shard_map/ppermute | solution.py:160
  88.0 1.9 %collective-permute-start.8 = (f32[32,40,3]{1,0,2:T(8,128)S(1)}, f32[32,40,3]{1,0,2:T(8,128)S(1)}, u32[]{:S(2)}, u32[]{:S(2)}) collective-permute-start(f32[32,40,3]{1,0,2:T(8,128)S(1)} %copy.18), channel_id=1, source_target_pairs={{0,1},{1,2},{2,3},{3,0},{4,5},{5,6},{6,7},{7,4},{8,9},{9,10},{10,1... | collective-permute-start | bytes 46088 | tf_op jit(solution)/shard_map/ppermute | solution.py:68
  90.8 5.1 %collective-permute-start.9 = (f32[32,40,3]{1,0,2:T(8,128)}, f32[32,40,3]{1,0,2:T(8,128)S(1)}, u32[]{:S(2)}, u32[]{:S(2)}) collective-permute-start(f32[32,40,3]{1,0,2:T(8,128)} %copy.20), channel_id=1, source_target_pairs={{1,0},{2,1},{3,2},{0,3},{5,4},{6,5},{7,6},{4,7},{9,8},{10,9},{11,1... | collective-permute-start | bytes 46088 | tf_op jit(solution)/shard_map/ppermute | solution.py:69
  96.1 1.2 copy.19
  97.5 1.2 copy.21
  98.6 13.0 %fusion.174 = f32[32,40,128]{2,1,0:T(8,128)S(1)} fusion(f32[32,52,128]{2,1,0:T(8,128)S(1)} %slice_bitcast_fusion, f32[32,40,128]{2,1,0:T(8,128)S(1)} %slice.1008, f32[32,40,3]{2,1,0:T(8,128)} %copy.21, f32[32,40,3]{2,1,0:T(8,128)} %copy.19, f32[5,32,52,128]{3,2,1,0:T(8,128)} %copy-done, f32[32,46,128]{2,1,0:T(8,128)S(1)} %fusion.21, ...), kind=kLoop, calls=%fused_computation.299 | loop fusion | flops 69632000 | bytes 8017920 | tf_op jit(solution)/shard_map/add | solution.py:193
  111.7 10.8 %collective-permute-start.10 = (f32[4,40,128]{2,1,0:T(8,128)S(1)}, f32[4,40,128]{2,1,0:T(8,128)S(1)}, u32[]{:S(2)}, u32[]{:S(2)}) collective-permute-start(f32[4,40,128]{2,1,0:T(8,128)S(1)} %get-tuple-element.48), channel_id=1, source_target_pairs={{0,16},{16,32},{32,48},{48,64},{64,80},{80,96},{96,112},{112,128},... | collective-permute-start | bytes 245768 | tf_op jit(solution)/shard_map/ppermute | solution.py:159
  122.5 1.9 %collective-permute-start.11 = (f32[4,40,128]{2,1,0:T(8,128)S(1)}, f32[4,40,128]{2,1,0:T(8,128)S(1)}, u32[]{:S(2)}, u32[]{:S(2)}) collective-permute-start(f32[4,40,128]{2,1,0:T(8,128)S(1)} %get-tuple-element.49), channel_id=1, source_target_pairs={{16,0},{32,16},{48,32},{64,48},{80,64},{96,80},{112,96},{128,112},... | collective-permute-start | bytes 245768 | tf_op jit(solution)/shard_map/ppermute | solution.py:160
  124.5 10.0 %collective-permute-done.11 = f32[4,40,128]{2,1,0:T(8,128)S(1)} collective-permute-done((f32[4,40,128]{2,1,0:T(8,128)S(1)}, f32[4,40,128]{2,1,0:T(8,128)S(1)}, u32[]{:S(2)}, u32[]{:S(2)}) %collective-permute-start.11) | collective-permute-done | bytes 81952 | tf_op jit(solution)/shard_map/ppermute | solution.py:160
  135.6 1.5 copy.22
  137.1 1.9 %collective-permute-start.12 = (f32[34,34,3]{1,0,2:T(8,128)S(1)}, f32[34,34,3]{1,0,2:T(8,128)S(1)}, u32[]{:S(2)}, u32[]{:S(2)}) collective-permute-start(f32[34,34,3]{1,0,2:T(8,128)S(1)} %copy.22), channel_id=1, source_target_pairs={{0,1},{1,2},{2,3},{3,0},{4,5},{5,6},{6,7},{7,4},{8,9},{9,10},{10,1... | collective-permute-start | bytes 41624 | tf_op jit(solution)/shard_map/ppermute | solution.py:68
  140.0 5.8 %collective-permute-start.13 = (f32[34,34,3]{1,0,2:T(8,128)}, f32[34,34,3]{1,0,2:T(8,128)S(1)}, u32[]{:S(2)}, u32[]{:S(2)}) collective-permute-start(f32[34,34,3]{1,0,2:T(8,128)} %copy.24), channel_id=1, source_target_pairs={{1,0},{2,1},{3,2},{0,3},{5,4},{6,5},{7,6},{4,7},{9,8},{10,9},{11,1... | collective-permute-start | bytes 41624 | tf_op jit(solution)/shard_map/ppermute | solution.py:69
  149.3 1.5 add_select_fusion
  151.2 13.2 %fusion.181 = f32[32,34,128]{2,1,0:T(8,128)S(1)} fusion(f32[34,34,3]{2,1,0:T(8,128)S(1)} %copy.25, f32[34,34,128]{2,1,0:T(8,128)S(1)} %copy-done.1, f32[34,34,3]{2,1,0:T(8,128)S(1)} %copy.23, f32[5,32,52,128]{3,2,1,0:T(8,128)} %copy-done, f32[32,40,128]{2,1,0:T(8,128)S(1)} %fusion.174, f32[4,40,128]{2,1,0:T(8,128)S(1)} %collective-permute-done.11, ...), kind=kLoop, calls=%fused_computation.308 | loop fusion | flops 59465728 | bytes 10936320 | tf_op jit(solution)/shard_map/jit(_where)/select_n | solution.py:206
  169.6 1.3 copy.26
  172.0 1.3 copy.27
  173.3 1.3 copy.28
  175.8 3.3 %all-to-all-start = ((f32[4,1,4096]{2,1,0:T(1,128)}), f32[4,1,4096]{2,1,0:T(1,128)S(1)}, u32[]{:S(2)}, u32[]{:S(2)}) async-start(f32[4,1,4096]{2,1,0:T(1,128)} %reshape.128), calls=%async_computation | async-start | bytes 131072 | tf_op jit(solution)/shard_map/all_to_all | solution.py:15
  180.0 3.7 %all-to-all-done = f32[4,1,4096]{2,1,0:T(1,128)S(1)} async-done(((f32[4,1,4096]{2,1,0:T(1,128)}), f32[4,1,4096]{2,1,0:T(1,128)S(1)}, u32[]{:S(2)}, u32[]{:S(2)}) %all-to-all-start) | async-done | bytes 65568 | tf_op jit(solution)/shard_map/all_to_all | solution.py:15
  (92 shorter events, 28.6 us)
Async XLA Ops:
  0.6 2.8 %copy-start.4 = (bf16[3,32,32,128]{3,2,1,0:T(8,128)(2,1)S(1)}, bf16[3,32,32,128]{3,2,1,0:T(8,128)(2,1)}, u32[]{:S(2)}) copy-start(bf16[3,32,32,128]{3,2,1,0:T(8,128)(2,1)} %param.5) | copy-start | bytes 2359300
  4.1 21.0 %collective-permute-start = (f32[5,32,10,128]{3,1,2,0:T(8,128)S(1)}, f32[5,32,10,128]{3,1,2,0:T(8,128)S(1)}, u32[]{:S(2)}, u32[]{:S(2)}) collective-permute-start(f32[5,32,10,128]{3,1,2,0:T(8,128)S(1)} %copy.10), channel_id=1, source_target_pairs={{0,4},{4,8},{8,12},{12,0},{1,5},{5,9},{9,13},{13,1},{2,6},{6,10},{... | collective-permute-start | bytes 2457608 | tf_op jit(solution)/shard_map/ppermute | solution.py:28
  7.6 20.7 %collective-permute-start.1 = (f32[5,32,10,128]{3,1,2,0:T(8,128)S(1)}, f32[5,32,10,128]{3,1,2,0:T(8,128)S(1)}, u32[]{:S(2)}, u32[]{:S(2)}) collective-permute-start(f32[5,32,10,128]{3,1,2,0:T(8,128)S(1)} %copy.11), channel_id=1, source_target_pairs={{4,0},{8,4},{12,8},{0,12},{5,1},{9,5},{13,9},{1,13},{6,2},{10,6},{... | collective-permute-start | bytes 2457608 | tf_op jit(solution)/shard_map/ppermute | solution.py:29
  29.4 2.1 %copy-start = (f32[5,32,52,128]{3,2,1,0:T(8,128)}, f32[5,32,52,128]{3,2,1,0:T(8,128)S(1)}, u32[]{:S(2)}) copy-start(f32[5,32,52,128]{3,2,1,0:T(8,128)S(1)} %pad_maximum_fusion) | copy-start | bytes 12779524
  33.4 23.0 %collective-permute-start.2 = (f32[7,46,128]{2,1,0:T(8,128)}, f32[7,46,128]{2,1,0:T(8,128)S(1)}, u32[]{:S(2)}, u32[]{:S(2)}) collective-permute-start(f32[7,46,128]{2,1,0:T(8,128)} %get-tuple-element.19), channel_id=1, source_target_pairs={{0,16},{16,32},{32,48},{48,64},{64,80},{80,96},{96,112},{112,128},... | collective-permute-start | bytes 494600 | tf_op jit(solution)/shard_map/ppermute | solution.py:188
  43.8 15.7 %collective-permute-start.3 = (f32[7,46,128]{2,1,0:T(8,128)}, f32[7,46,128]{2,1,0:T(8,128)}, u32[]{:S(2)}, u32[]{:S(2)}) collective-permute-start(f32[7,46,128]{2,1,0:T(8,128)} %get-tuple-element.18), channel_id=1, source_target_pairs={{16,0},{32,16},{48,32},{64,48},{80,64},{96,80},{112,96},{128,112},... | collective-permute-start | bytes 494600 | tf_op jit(solution)/shard_map/ppermute | solution.py:189
  46.4 7.5 %collective-permute-start.4 = (f32[32,46,3]{1,0,2:T(8,128)S(1)}, f32[32,46,3]{1,0,2:T(8,128)S(1)}, u32[]{:S(2)}, u32[]{:S(2)}) collective-permute-start(f32[32,46,3]{1,0,2:T(8,128)S(1)} %copy.14), channel_id=1, source_target_pairs={{0,1},{1,2},{2,3},{3,0},{4,5},{5,6},{6,7},{7,4},{8,9},{9,10},{10,1... | collective-permute-start | bytes 53000 | tf_op jit(solution)/shard_map/ppermute | solution.py:68
  49.4 5.8 %collective-permute-start.5 = (f32[32,46,3]{1,0,2:T(8,128)S(1)}, f32[32,46,3]{1,0,2:T(8,128)S(1)}, u32[]{:S(2)}, u32[]{:S(2)}) collective-permute-start(f32[32,46,3]{1,0,2:T(8,128)S(1)} %copy.16), channel_id=1, source_target_pairs={{1,0},{2,1},{3,2},{0,3},{5,4},{6,5},{7,6},{4,7},{9,8},{10,9},{11,1... | collective-permute-start | bytes 53000 | tf_op jit(solution)/shard_map/ppermute | solution.py:69
  75.4 23.2 %collective-permute-start.6 = (f32[3,40,128]{2,1,0:T(8,128)S(1)}, f32[3,40,128]{2,1,0:T(8,128)S(1)}, u32[]{:S(2)}, u32[]{:S(2)}) collective-permute-start(f32[3,40,128]{2,1,0:T(8,128)S(1)} %get-tuple-element.39), channel_id=1, source_target_pairs={{0,16},{16,32},{32,48},{48,64},{64,80},{80,96},{96,112},{112,128},... | collective-permute-start | bytes 184328 | tf_op jit(solution)/shard_map/ppermute | solution.py:159
  85.5 13.1 %collective-permute-start.7 = (f32[3,40,128]{2,1,0:T(8,128)S(1)}, f32[3,40,128]{2,1,0:T(8,128)S(1)}, u32[]{:S(2)}, u32[]{:S(2)}) collective-permute-start(f32[3,40,128]{2,1,0:T(8,128)S(1)} %get-tuple-element.38), channel_id=1, source_target_pairs={{16,0},{32,16},{48,32},{64,48},{80,64},{96,80},{112,96},{128,112},... | collective-permute-start | bytes 184328 | tf_op jit(solution)/shard_map/ppermute | solution.py:160
  88.0 8.1 %collective-permute-start.8 = (f32[32,40,3]{1,0,2:T(8,128)S(1)}, f32[32,40,3]{1,0,2:T(8,128)S(1)}, u32[]{:S(2)}, u32[]{:S(2)}) collective-permute-start(f32[32,40,3]{1,0,2:T(8,128)S(1)} %copy.18), channel_id=1, source_target_pairs={{0,1},{1,2},{2,3},{3,0},{4,5},{5,6},{6,7},{7,4},{8,9},{9,10},{10,1... | collective-permute-start | bytes 46088 | tf_op jit(solution)/shard_map/ppermute | solution.py:68
  90.8 6.6 %collective-permute-start.9 = (f32[32,40,3]{1,0,2:T(8,128)}, f32[32,40,3]{1,0,2:T(8,128)S(1)}, u32[]{:S(2)}, u32[]{:S(2)}) collective-permute-start(f32[32,40,3]{1,0,2:T(8,128)} %copy.20), channel_id=1, source_target_pairs={{1,0},{2,1},{3,2},{0,3},{5,4},{6,5},{7,6},{4,7},{9,8},{10,9},{11,1... | collective-permute-start | bytes 46088 | tf_op jit(solution)/shard_map/ppermute | solution.py:69
  111.7 12.8 %collective-permute-start.10 = (f32[4,40,128]{2,1,0:T(8,128)S(1)}, f32[4,40,128]{2,1,0:T(8,128)S(1)}, u32[]{:S(2)}, u32[]{:S(2)}) collective-permute-start(f32[4,40,128]{2,1,0:T(8,128)S(1)} %get-tuple-element.48), channel_id=1, source_target_pairs={{0,16},{16,32},{32,48},{48,64},{64,80},{80,96},{96,112},{112,128},... | collective-permute-start | bytes 245768 | tf_op jit(solution)/shard_map/ppermute | solution.py:159
  122.5 12.0 %collective-permute-start.11 = (f32[4,40,128]{2,1,0:T(8,128)S(1)}, f32[4,40,128]{2,1,0:T(8,128)S(1)}, u32[]{:S(2)}, u32[]{:S(2)}) collective-permute-start(f32[4,40,128]{2,1,0:T(8,128)S(1)} %get-tuple-element.49), channel_id=1, source_target_pairs={{16,0},{32,16},{48,32},{64,48},{80,64},{96,80},{112,96},{128,112},... | collective-permute-start | bytes 245768 | tf_op jit(solution)/shard_map/ppermute | solution.py:160
  134.5 11.3 %copy-start.5 = (s32[4]{0:T(128)S(1)}, s32[4]{0:T(128)}, u32[]{:S(2)}) copy-start(s32[4]{0:T(128)} %param.7) | copy-start | bytes 52
  137.1 11.5 %collective-permute-start.12 = (f32[34,34,3]{1,0,2:T(8,128)S(1)}, f32[34,34,3]{1,0,2:T(8,128)S(1)}, u32[]{:S(2)}, u32[]{:S(2)}) collective-permute-start(f32[34,34,3]{1,0,2:T(8,128)S(1)} %copy.22), channel_id=1, source_target_pairs={{0,1},{1,2},{2,3},{3,0},{4,5},{5,6},{6,7},{7,4},{8,9},{9,10},{10,1... | collective-permute-start | bytes 41624 | tf_op jit(solution)/shard_map/ppermute | solution.py:68
  140.0 8.9 %collective-permute-start.13 = (f32[34,34,3]{1,0,2:T(8,128)}, f32[34,34,3]{1,0,2:T(8,128)S(1)}, u32[]{:S(2)}, u32[]{:S(2)}) collective-permute-start(f32[34,34,3]{1,0,2:T(8,128)} %copy.24), channel_id=1, source_target_pairs={{1,0},{2,1},{3,2},{0,3},{5,4},{6,5},{7,6},{4,7},{9,8},{10,9},{11,1... | collective-permute-start | bytes 41624 | tf_op jit(solution)/shard_map/ppermute | solution.py:69
  149.3 1.5 copy-start.1
  164.4 0.8 copy-start.2
  172.0 7.1 %copy-start.3 = (f32[32,34,128]{2,1,0:T(8,128)S(1)}, f32[32,34,128]{2,1,0:T(8,128)}, u32[]{:S(2)}) copy-start(f32[32,34,128]{2,1,0:T(8,128)} %copy-done.2) | copy-start | bytes 1671172
  175.8 7.9 %all-to-all-start = ((f32[4,1,4096]{2,1,0:T(1,128)}), f32[4,1,4096]{2,1,0:T(1,128)S(1)}, u32[]{:S(2)}, u32[]{:S(2)}) async-start(f32[4,1,4096]{2,1,0:T(1,128)} %reshape.128), calls=%async_computation | async-start | bytes 131072 | tf_op jit(solution)/shard_map/all_to_all | solution.py:15
